TPU v7x, 512 devices: a whole 4x4x16 slice. The times are simulated.
512 devices in a mesh: seq: 32 (over x, y, core), mp: 16 (over z).
Axes of the slice: x: 4, y: 4, z: 16, core: 2. Of those that a mesh axis runs over, the one named last changes fastest.
Arguments:
- token_ids: int32 [256, 4], replicated, may hold values from 0 to 151935
- embedding: bfloat16 [151936, 1536], P('seq', 'mp'), may hold values from -13 to 13
- attn_gain: float32 [1536], P('mp'), may hold values from 0.25 to 1.75
- w_qkv: bfloat16 [1536, 2048], P('mp', 'seq'), may hold values from -0.15625 to 0.15625
- w_out: bfloat16 [1536, 1536], P('seq', 'mp'), may hold values from -0.15625 to 0.15625
- prompt_cache: bfloat16 [2, 32, 2048, 256], P(None, 'mp', 'seq'), may hold values from -170 to 170
- request_cache: bfloat16 [2, 256, 2048, 256], P(None, 'mp', 'seq'), may hold values from -170 to 170
- group_ids: int32 [256], P('mp'), may hold values from 0 to 1
- prefix_len: int32 [32], P('mp'), may hold values from 1 to 2048
- suffix_len: int32 [256], P('mp'), may hold values from 0 to 2048
- moe_gain: float32 [1536], replicated, may hold values from 0.25 to 1.75
- w_router: bfloat16 [1536, 32], replicated, may hold values from -0.15625 to 0.15625
- w_gate_up: bfloat16 [32, 2, 768, 1536], P('seq', None, 'mp'), may hold values from -0.15625 to 0.15625
- w_down: bfloat16 [32, 768, 1536], P('seq', 'mp'), may hold values from -0.21875 to 0.21875
- routes: int32 [256, 4, 4], replicated, may hold values from 0 to 31, all different within a row; in each aligned block of 32 rows (0 to 31, 32 to 63, ..., all dimensions but the last counted through in order) at most 8 rows name the same one
Outputs:
- hidden_out: bfloat16 [256, 4, 1536], P('seq', None, 'mp')
Inputs may be any that keep to these rules, and one draw needn't show every extreme that they name: `routes`: in each aligned block of 32 rows (request, step) taken in order, the requests of one index of seq, no expert is named more than 8 times.
All inputs are finite; a program needn't handle non-finite values.
Results may differ from a plain program's by a relative error of at most 0.015.
The roundings to bfloat16 on the way count: a program that leaves them out, or rounds other values in their place, can miss the bound.
Values may be sent and summed in bfloat16 or wider, within the bound.
No kernel may reach another device: no remote copies, remote signals or barrier semaphores. Data moves between devices by JAX's collectives and lax.ppermute only.
A program may use at most 128 MiB of HBM per device.

v0:
```python
import math
import numpy as np
import jax
import jax.numpy as jnp
from jax import lax
from jax.sharding import PartitionSpec as P

D = 1536
QUERY_HEADS = 12
KEY_VALUE_HEADS = 2
HEAD_SIZE = 128
E = 32
TOPK = 4
NEW_TOKENS = 4
MOST = 8
EPS = 1e-06
NEG = -1e30


def exchange(values, axis):
    return lax.all_to_all(values, axis, 0, 0, tiled=True)


def on_device(
    token_ids,
    embedding,
    attn_gain,
    w_qkv,
    w_out,
    prompt_cache,
    request_cache,
    group_ids,
    prefix_len,
    suffix_len,
    moe_gain,
    w_router,
    w_gate_up,
    w_down,
    routes,
):
    n_seq = lax.axis_size("seq")
    n_mp = lax.axis_size("mp")
    s = lax.axis_index("seq")
    total_rows = token_ids.shape[0] * NEW_TOKENS
    home_rows = total_rows // n_seq
    feat_mp = embedding.shape[1]
    vocab_rows = embedding.shape[0]
    local_ids = token_ids.reshape(total_rows) - s * vocab_rows
    inside = (local_ids >= 0) & (local_ids < vocab_rows)
    looked = jnp.take(embedding, jnp.clip(local_ids, 0, vocab_rows - 1), axis=0)
    looked = jnp.where(inside[:, None], looked, jnp.zeros_like(looked))
    got = exchange(looked.reshape(n_seq, home_rows, feat_mp), "seq")
    x_home = jnp.sum(got.astype(jnp.float32), axis=0)
    square_sum = lax.psum(jnp.sum(x_home * x_home, axis=-1), "mp")
    normed = (x_home * lax.rsqrt(square_sum[:, None] / D + EPS) * attn_gain).astype(jnp.bfloat16)
    normed_all = lax.all_gather(normed, "seq", axis=0, tiled=True)
    qkv_part = jnp.dot(normed_all, w_qkv, preferred_element_type=jnp.float32)
    attn_rows = total_rows // n_mp
    qkv_got = exchange(qkv_part.reshape(n_mp, attn_rows, qkv_part.shape[-1]), "mp")
    qkv_cols = jnp.sum(qkv_got, axis=0).astype(jnp.bfloat16)
    qkv_rows = lax.all_gather(qkv_cols, "seq", axis=1, tiled=True)
    request_count = group_ids.shape[0]
    groups_per = QUERY_HEADS // KEY_VALUE_HEADS
    qf = QUERY_HEADS * HEAD_SIZE
    kf = KEY_VALUE_HEADS * HEAD_SIZE
    q = qkv_rows[:, :qf].reshape(request_count, NEW_TOKENS, KEY_VALUE_HEADS, groups_per, HEAD_SIZE)
    k_new = qkv_rows[:, qf : qf + kf].reshape(request_count, NEW_TOKENS, KEY_VALUE_HEADS, HEAD_SIZE)
    v_new = qkv_rows[:, qf + kf :].reshape(request_count, NEW_TOKENS, KEY_VALUE_HEADS, HEAD_SIZE)
    pre_rows = prompt_cache.shape[2]
    suf_rows = request_cache.shape[2]
    first_group = (group_ids == 0)[:, None, None]
    pre_k = jnp.where(first_group, prompt_cache[0, 0][None], prompt_cache[0, 1][None])
    pre_v = jnp.where(first_group, prompt_cache[1, 0][None], prompt_cache[1, 1][None])
    keys = jnp.concatenate([pre_k, request_cache[0]], axis=1).reshape(
        request_count, pre_rows + suf_rows, KEY_VALUE_HEADS, HEAD_SIZE
    )
    values = jnp.concatenate([pre_v, request_cache[1]], axis=1).reshape(
        request_count, pre_rows + suf_rows, KEY_VALUE_HEADS, HEAD_SIZE
    )
    own_prefix = jnp.where(group_ids == 0, prefix_len[0], prefix_len[1])
    pre_pos = s * pre_rows + jnp.arange(pre_rows, dtype=jnp.int32)
    suf_pos = s * suf_rows + jnp.arange(suf_rows, dtype=jnp.int32)
    valid = jnp.concatenate(
        [pre_pos[None, :] < own_prefix[:, None], suf_pos[None, :] < suffix_len[:, None]], axis=1
    )[:, None, None, None, :]
    score_scale = 1.0 / math.sqrt(HEAD_SIZE)
    scores = (
        jnp.einsum("jtkgd,jpkd->jtkgp", q, keys, preferred_element_type=jnp.float32) * score_scale
    )
    scores = jnp.where(valid, scores, NEG)
    block_max = jnp.max(scores, axis=-1)
    probs = jnp.where(valid, jnp.exp(scores - block_max[..., None]), 0.0)
    block_sum = jnp.sum(probs, axis=-1)
    block_acc = jnp.einsum(
        "jtkgp,jpkd->jtkgd", probs.astype(jnp.bfloat16), values, preferred_element_type=jnp.float32
    )
    new_scores = (
        jnp.einsum("jtkgd,jukd->jtkgu", q, k_new, preferred_element_type=jnp.float32) * score_scale
    )
    causal = (jnp.arange(NEW_TOKENS)[:, None] >= jnp.arange(NEW_TOKENS)[None, :])[
        None, :, None, None, :
    ]
    new_scores = jnp.where(causal, new_scores, NEG)
    new_max = jnp.max(new_scores, axis=-1)
    new_probs = jnp.where(causal, jnp.exp(new_scores - new_max[..., None]), 0.0)
    new_sum = jnp.sum(new_probs, axis=-1)
    new_acc = jnp.einsum(
        "jtkgu,jukd->jtkgd",
        new_probs.astype(jnp.bfloat16),
        v_new,
        preferred_element_type=jnp.float32,
    )
    fs = qf // n_seq
    acc_flat = block_acc.reshape(attn_rows, qf)
    acc_parts = acc_flat.reshape(attn_rows, n_seq, fs).transpose(1, 0, 2)
    head_pick = np.array(
        [[i * fs // HEAD_SIZE, (i * fs + fs - 1) // HEAD_SIZE] for i in range(n_seq)]
    )
    max_flat = block_max.reshape(attn_rows, QUERY_HEADS)
    sum_flat = block_sum.reshape(attn_rows, QUERY_HEADS)
    max_parts = max_flat[:, head_pick].transpose(1, 0, 2)
    sum_parts = sum_flat[:, head_pick].transpose(1, 0, 2)
    merged = exchange(jnp.concatenate([acc_parts, max_parts, sum_parts], axis=-1), "seq")
    got_acc = merged[..., :fs]
    feat_ids = s * fs + jnp.arange(fs, dtype=jnp.int32)
    second = feat_ids // HEAD_SIZE - s * fs // HEAD_SIZE == 1
    got_max = jnp.where(second, merged[..., fs + 1 : fs + 2], merged[..., fs : fs + 1])
    got_sum = jnp.where(second, merged[..., fs + 3 : fs + 4], merged[..., fs + 2 : fs + 3])
    own_heads = feat_ids // HEAD_SIZE
    n_max = jnp.take(new_max.reshape(attn_rows, QUERY_HEADS), own_heads, axis=1)
    n_sum = jnp.take(new_sum.reshape(attn_rows, QUERY_HEADS), own_heads, axis=1)
    n_acc = lax.dynamic_slice_in_dim(new_acc.reshape(attn_rows, qf), s * fs, fs, 1)
    overall = jnp.maximum(jnp.max(got_max, axis=0), n_max)
    cache_weight = jnp.exp(got_max - overall)
    own_weight = jnp.exp(n_max - overall)
    denominator = jnp.sum(cache_weight * got_sum, axis=0) + own_weight * n_sum
    numerator = jnp.sum(cache_weight * got_acc, axis=0) + own_weight * n_acc
    attended = (numerator / denominator).astype(jnp.bfloat16)
    att_all = lax.all_gather(attended, "mp", axis=0, tiled=True)
    out_part = jnp.dot(att_all, w_out, preferred_element_type=jnp.float32)
    out_got = exchange(out_part.reshape(n_seq, home_rows, out_part.shape[-1]), "seq")
    x2 = (x_home + jnp.sum(out_got, axis=0)).astype(jnp.bfloat16)
    route_blocks = routes.reshape(n_seq, home_rows, TOPK)
    experts_all = jnp.arange(E, dtype=jnp.int32)
    hit = jnp.any(route_blocks[:, :, :, None] == experts_all, axis=2)
    hit_count = hit.astype(jnp.int32)
    ahead = jnp.cumsum(hit_count, axis=1) - hit_count
    chosen = hit[..., None] & (ahead[..., None] == jnp.arange(MOST, dtype=jnp.int32))
    chosen = jnp.transpose(chosen, (0, 2, 3, 1)).astype(jnp.bfloat16)
    member = hit.astype(jnp.bfloat16)
    home_table = chosen[s]
    dispatch = jnp.einsum("esr,rf->esf", home_table, x2, preferred_element_type=jnp.float32).astype(
        jnp.bfloat16
    )
    slot_rows = exchange(dispatch, "seq")
    slot_full = lax.all_gather(slot_rows, "mp", axis=2, tiled=True).reshape(n_seq * MOST, D)
    expert = s
    expert_table = chosen[:, expert]
    slot_member = jnp.einsum(
        "bsr,bre->bse", expert_table, member, preferred_element_type=jnp.float32
    ).reshape(n_seq * MOST, E)
    floats2 = slot_full.astype(jnp.float32)
    mean_sq = jnp.mean(floats2 * floats2, axis=-1, keepdims=True)
    normed2 = (floats2 * lax.rsqrt(mean_sq + EPS) * moe_gain).astype(jnp.bfloat16)
    logits = jnp.dot(normed2, w_router, preferred_element_type=jnp.float32)
    which = (experts_all == expert).astype(jnp.float32)
    own_flag = jnp.sum(slot_member * which, axis=1)
    own_logit = jnp.sum(logits * which, axis=1)
    denom = jnp.sum(jnp.where(slot_member > 0, jnp.exp(logits), 0.0), axis=1)
    share = own_flag * jnp.exp(own_logit) / (denom + 1.0 - own_flag)
    gate_up = w_gate_up[0]
    half = gate_up.shape[1]
    both = lax.dot_general(
        normed2,
        gate_up.reshape(2 * half, D),
        (((1,), (1,)), ((), ())),
        preferred_element_type=jnp.float32,
    )
    hidden = (jnp.maximum(both[:, :half], 0.0) * both[:, half:]).astype(jnp.bfloat16)
    down_part = jnp.dot(hidden, w_down[0], preferred_element_type=jnp.float32).astype(jnp.bfloat16)
    down_got = exchange(down_part.reshape(n_seq * MOST, n_mp, feat_mp).transpose(1, 0, 2), "mp")
    expert_out = jnp.sum(down_got.astype(jnp.float32), axis=0).astype(jnp.bfloat16)
    weighted = (share[:, None] * expert_out.astype(jnp.float32)).astype(jnp.bfloat16)
    back = exchange(weighted.reshape(n_seq, MOST, feat_mp), "seq")
    terms = jnp.einsum("esr,esf->rf", home_table, back, preferred_element_type=jnp.float32)
    final = (x2.astype(jnp.float32) + terms).astype(jnp.bfloat16)
    return final.reshape(home_rows // NEW_TOKENS, NEW_TOKENS, feat_mp)


def solution(mesh):
    in_specs = (
        P(),
        P("seq", "mp"),
        P("mp"),
        P("mp", "seq"),
        P("seq", "mp"),
        P(None, "mp", "seq", None),
        P(None, "mp", "seq", None),
        P("mp"),
        P("mp"),
        P("mp"),
        P(),
        P(),
        P("seq", None, "mp", None),
        P("seq", "mp", None),
        P(),
    )
    out_specs = P("seq", None, "mp")
    return jax.shard_map(
        on_device, mesh=mesh, in_specs=in_specs, out_specs=out_specs, check_vma=False
    )
```

profile of v0, /device:TPU:1, one launch (start us, length us, event | category | flops | bytes accessed | tf_op | source)
XLA Modules:
  0.0 341.7 jit_solution(17688282065486856965)
XLA Ops:
  0.0 0.7 compare_and_fusion.1
  0.7 0.7 subtract_clamp_fusion
  2.2 2.2 copy.150
  4.4 3.2 gather_fusion
  7.6 1.0 select_select_fusion
  8.6 10.5 %all-to-all-start = ((bf16[32,32,96]{2,1,0:T(8,128)(2,1)}), bf16[32,32,96]{2,1,0:T(8,128)(2,1)S(1)}, u32[]{:S(2)}, u32[]{:S(2)}) async-start(bf16[32,32,96]{2,1,0:T(8,128)(2,1)} %select_select_fusion), calls=%async_computation | async-start | bytes 524288 | tf_op jit(solution)/shard_map/all_to_all | solution.py:21
  20.8 0.8 fusion.1
  21.6 1.1 copy.194
  24.2 1.3 copy.196
  26.4 1.2 broadcast_select_fusion.2
  28.4 27.4 %psum.7 = f32[32]{0:T(128)S(1)} all-reduce(f32[32]{0:T(128)S(1)} %multiply_reduce_fusion.2), channel_id=1, replica_groups=mesh['seq'=32,'mp'=16] {'mp'}, use_global_device_ids=true, to_apply=%region_2.3 | all-reduce | flops 32 | bytes 256 | tf_op jit(solution)/shard_map/psum | solution.py:54
  55.8 32.0 %all_gather.12 = bf16[1024,96]{1,0:T(8,128)(2,1)S(1)} all-gather(bf16[32,96]{1,0:T(8,128)(2,1)S(1)} %multiply_convert_fusion), channel_id=1, replica_groups=mesh['seq'=32,'mp'=16] {'seq'}, dimensions={0}, use_global_device_ids=true | all-gather | bytes 202752 | tf_op jit(solution)/shard_map/all_gather | solution.py:56
  88.4 1.0 reshape.313
  89.5 6.4 %all-to-all-start.1 = ((f32[16,1,4096]{2,1,0:T(1,128)}), f32[16,1,4096]{2,1,0:T(1,128)S(1)}, u32[]{:S(2)}, u32[]{:S(2)}) async-start(f32[16,1,4096]{2,1,0:T(1,128)} %reshape.313), calls=%async_computation.1 | async-start | bytes 524288 | tf_op jit(solution)/shard_map/all_to_all | solution.py:21
  96.8 13.2 %all-to-all-done.1 = f32[16,1,4096]{2,1,0:T(1,128)S(1)} async-done(((f32[16,1,4096]{2,1,0:T(1,128)}), f32[16,1,4096]{2,1,0:T(1,128)S(1)}, u32[]{:S(2)}, u32[]{:S(2)}) %all-to-all-start.1) | async-done | bytes 262176 | tf_op jit(solution)/shard_map/all_to_all | solution.py:21
  110.5 1.2 reduce.3
  111.9 29.1 %all_gather.13 = bf16[64,2048]{0,1:T(8,128)(2,1)S(1)} all-gather(bf16[64,64]{0,1:T(8,128)(2,1)S(1)} %bitcast_reduce_fusion), channel_id=1, replica_groups=mesh['seq'=32,'mp'=16] {'seq'}, dimensions={1}, use_global_device_ids=true | all-gather | bytes 270336 | tf_op jit(solution)/shard_map/all_gather | solution.py:61
  141.4 0.6 reshape.243
  142.3 0.8 fusion.76
  146.5 1.0 copy.167
  147.4 1.0 copy.164
  148.4 1.6 pad_maximum_fusion
  150.0 1.8 copy.168
  151.9 1.3 reshape.315
  153.2 4.4 %all-to-all-start.2 = ((f32[32,1,3328]{2,1,0:T(1,128)}), f32[32,1,3328]{2,1,0:T(1,128)S(1)}, u32[]{:S(2)}, u32[]{:S(2)}) async-start(f32[32,1,3328]{2,1,0:T(1,128)} %reshape.315), calls=%async_computation.2 | async-start | bytes 851968 | tf_op jit(solution)/shard_map/all_to_all | solution.py:21
  157.6 1.3 fusion.77
  160.2 0.7 gather_fusion.4
  160.9 0.7 gather_fusion.3
  162.2 5.9 %all-to-all-done.2 = f32[32,1,3328]{2,1,0:T(1,128)S(1)} async-done(((f32[32,1,3328]{2,1,0:T(1,128)}), f32[32,1,3328]{2,1,0:T(1,128)S(1)}, u32[]{:S(2)}, u32[]{:S(2)}) %all-to-all-start.2) | async-done | bytes 426016 | tf_op jit(solution)/shard_map/all_to_all | solution.py:21
  168.2 1.5 reduce.4
  170.8 24.4 %all-gather = bf16[16,64,48]{1,2,0:T(8,128)(2,1)S(1)} all-gather(bf16[1,64,48]{1,2,0:T(8,128)(2,1)S(1)} %fusion.63), channel_id=1, replica_groups=mesh['seq'=32,'mp'=16] {'mp'}, dimensions={0}, use_global_device_ids=true | all-gather | bytes 104448 | tf_op jit(solution)/shard_map/all_gather | solution.py:139
  195.5 1.1 fusion.79
  196.6 10.6 %all-to-all-start.3 = ((f32[32,32,96]{2,1,0:T(8,128)}), f32[32,32,96]{2,1,0:T(8,128)S(1)}, u32[]{:S(2)}, u32[]{:S(2)}) async-start(f32[32,32,96]{2,1,0:T(8,128)} %bitcast.26), calls=%async_computation.3 | async-start | bytes 1048576 | tf_op jit(solution)/shard_map/all_to_all | solution.py:21
  207.3 0.9 fusion
  208.2 0.9 copy-done.5
  209.3 9.6 %all-to-all-done.3 = f32[32,32,96]{2,1,0:T(8,128)S(1)} async-done(((f32[32,32,96]{2,1,0:T(8,128)}), f32[32,32,96]{2,1,0:T(8,128)S(1)}, u32[]{:S(2)}, u32[]{:S(2)}) %all-to-all-start.3) | async-done | bytes 393248 | tf_op jit(solution)/shard_map/all_to_all | solution.py:21
  219.2 10.8 %all_to_all.35 = bf16[32,8,96]{2,1,0:T(8,128)(2,1)S(1)} all-to-all(bf16[32,8,96]{2,1,0:T(8,128)(2,1)S(1)} %copy.198), channel_id=1, replica_groups=mesh['seq'=32,'mp'=16] {'seq'}, dimensions={0} | all-to-all | bytes 98304 | tf_op jit(solution)/shard_map/all_to_all | solution.py:21
  229.9 0.8 copy.199
  230.8 45.7 %all_gather.15 = bf16[32,8,1536]{0,1,2:T(8,128)(2,1)S(1)} all-gather(bf16[32,8,96]{0,1,2:T(8,128)(2,1)} %copy.199), channel_id=1, replica_groups=mesh['seq'=32,'mp'=16] {'mp'}, dimensions={2}, use_global_device_ids=true | all-gather | bytes 835584 | tf_op jit(solution)/shard_map/all_gather | solution.py:156
  276.5 3.6 %copy.200 = bf16[32,8,1536]{2,1,0:T(8,128)(2,1)} copy(bf16[32,8,1536]{0,1,2:T(8,128)(2,1)S(1)} %all_gather.15) | data formatting | bytes 1572864 | tf_op jit(solution)/shard_map/all_gather | solution.py:156
  280.1 1.4 fusion.5
  281.7 1.6 fusion.24
  283.7 1.2 copy.205
  284.9 5.1 %all-to-all-start.5 = ((bf16[16,256,96]{1,2,0:T(8,128)(2,1)}), bf16[16,256,96]{1,2,0:T(8,128)(2,1)S(1)}, u32[]{:S(2)}, u32[]{:S(2)}) async-start(bf16[16,256,96]{1,2,0:T(8,128)(2,1)} %bitcast.39), calls=%async_computation.5 | async-start | bytes 1572864 | tf_op jit(solution)/shard_map/all_to_all | solution.py:21
  290.0 1.0 multiply_reduce_fusion
  292.0 29.6 %all-to-all-done.5 = bf16[16,256,96]{1,2,0:T(8,128)(2,1)S(1)} async-done(((bf16[16,256,96]{1,2,0:T(8,128)(2,1)}), bf16[16,256,96]{1,2,0:T(8,128)(2,1)S(1)}, u32[]{:S(2)}, u32[]{:S(2)}) %all-to-all-start.5) | async-done | bytes 786464 | tf_op jit(solution)/shard_map/all_to_all | solution.py:21
  321.8 19.1 %all_to_all.36 = bf16[32,8,96]{2,1,0:T(8,128)(2,1)S(1)} all-to-all(bf16[32,8,96]{2,1,0:T(8,128)(2,1)S(1)} %fusion.46), channel_id=1, replica_groups=mesh['seq'=32,'mp'=16] {'seq'}, dimensions={0} | all-to-all | bytes 98304 | tf_op jit(solution)/shard_map/all_to_all | solution.py:21
  340.9 0.8 fusion.13
  (158 shorter events, 16.8 us)
Async XLA Ops:
  0.0 281.7 %copy-start = (bf16[1,2,48,1536]{3,2,1,0:T(8,128)(2,1)S(1)}, bf16[1,2,48,1536]{3,2,1,0:T(8,128)(2,1)}, u32[]{:S(2)}) copy-start(bf16[1,2,48,1536]{3,2,1,0:T(8,128)(2,1)} %param.32) | copy-start | bytes 884740
  4.4 16.0 %copy-start.13 = (s32[256,4,4]{0,2,1:T(4,128)S(1)}, s32[256,4,4]{0,2,1:T(4,128)}, u32[]{:S(2)}) copy-start(s32[256,4,4]{0,2,1:T(4,128)} %param.34) | copy-start | bytes 49156
  8.6 14.8 %copy-start.19 = (s32[2]{0:T(128)S(1)}, s32[2]{0:T(128)}, u32[]{:S(2)}) copy-start(s32[2]{0:T(128)} %param.28) | copy-start | bytes 28
  8.6 15.4 %copy-start.11 = (bf16[2,2,64,256]{3,2,1,0:T(8,128)(2,1)S(1)}, bf16[2,2,64,256]{3,2,1,0:T(8,128)(2,1)}, u32[]{:S(2)}) copy-start(bf16[2,2,64,256]{3,2,1,0:T(8,128)(2,1)} %param.25) | copy-start | bytes 393220
  8.6 19.6 %all-to-all-start = ((bf16[32,32,96]{2,1,0:T(8,128)(2,1)}), bf16[32,32,96]{2,1,0:T(8,128)(2,1)S(1)}, u32[]{:S(2)}, u32[]{:S(2)}) async-start(bf16[32,32,96]{2,1,0:T(8,128)(2,1)} %select_select_fusion), calls=%async_computation | async-start | bytes 524288 | tf_op jit(solution)/shard_map/all_to_all | solution.py:21
  20.7 4.7 %copy-start.6 = (bf16[2,16,64,256]{3,2,1,0:T(8,128)(2,1)S(1)}, bf16[2,16,64,256]{3,2,1,0:T(8,128)(2,1)}, u32[]{:S(2)}) copy-start(bf16[2,16,64,256]{3,2,1,0:T(8,128)(2,1)} %param.26) | copy-start | bytes 3145732
  21.6 2.6 copy-start.3
  25.7 0.7 copy-start.22
  25.8 30.0 %copy-start.20 = (f32[96]{0:T(128)S(1)}, f32[96]{0:T(128)}, u32[]{:S(2)}) copy-start(f32[96]{0:T(128)} %param.22) | copy-start | bytes 1156
  25.9 62.0 %copy-start.14 = (bf16[96,64]{0,1:T(8,128)(2,1)S(1)}, bf16[96,64]{0,1:T(8,128)(2,1)}, u32[]{:S(2)}) copy-start(bf16[96,64]{0,1:T(8,128)(2,1)} %param.23) | copy-start | bytes 36868
  88.1 7.8 %copy-start.23 = (s32[16]{0:T(128)S(1)}, s32[16]{0:T(128)}, u32[]{:S(2)}) copy-start(s32[16]{0:T(128)} %param.29) | copy-start | bytes 196
  88.1 8.5 %copy-start.21 = (s32[64]{0:T(128)S(1)}, s32[64]{0:T(128)}, u32[]{:S(2)}) copy-start(s32[64]{0:T(128)} %constant.117) | copy-start | bytes 772
  89.5 20.6 %all-to-all-start.1 = ((f32[16,1,4096]{2,1,0:T(1,128)}), f32[16,1,4096]{2,1,0:T(1,128)S(1)}, u32[]{:S(2)}, u32[]{:S(2)}) async-start(f32[16,1,4096]{2,1,0:T(1,128)} %reshape.313), calls=%async_computation.1 | async-start | bytes 524288 | tf_op jit(solution)/shard_map/all_to_all | solution.py:21
  142.2 1.6 copy-start.8
  151.9 5.7 %copy-start.9 = (bf16[16,4,2,6,128]{4,3,2,1,0:T(8,128)(2,1)S(1)}, bf16[16,4,2,6,128]{4,3,2,1,0:T(8,128)(2,1)}, u32[]{:S(2)}) copy-start(bf16[16,4,2,6,128]{4,3,2,1,0:T(8,128)(2,1)} %copy-done.8) | copy-start | bytes 589828
  151.9 5.7 %copy-start.12 = (bf16[16,4,2,128]{3,2,1,0:T(2,128)(2,1)S(1)}, bf16[16,4,2,128]{3,2,1,0:T(2,128)(2,1)}, u32[]{:S(2)}) copy-start(bf16[16,4,2,128]{3,2,1,0:T(2,128)(2,1)} %reshape.243) | copy-start | bytes 98308
  151.9 5.7 %copy-start.17 = (pred[4,4]{1,0:T(4,128)(4,1)S(1)}, pred[4,4]{1,0:T(4,128)(4,1)}, u32[]{:S(2)}) copy-start(pred[4,4]{1,0:T(4,128)(4,1)} %iota_compare_fusion.2) | copy-start | bytes 52
  153.2 15.0 %all-to-all-start.2 = ((f32[32,1,3328]{2,1,0:T(1,128)}), f32[32,1,3328]{2,1,0:T(1,128)S(1)}, u32[]{:S(2)}, u32[]{:S(2)}) async-start(f32[32,1,3328]{2,1,0:T(1,128)} %reshape.315), calls=%async_computation.2 | async-start | bytes 851968 | tf_op jit(solution)/shard_map/all_to_all | solution.py:21
  162.0 8.1 %copy-start.18 = (pred[48]{0:T(512)(128)(4,1)S(1)}, pred[48]{0:T(512)(128)(4,1)}, u32[]{:S(2)}) copy-start(pred[48]{0:T(512)(128)(4,1)} %subtract_compare_fusion) | copy-start | bytes 148
  162.0 8.3 %copy-start.16 = (pred[48]{0:T(512)(128)(4,1)S(1)}, pred[48]{0:T(512)(128)(4,1)}, u32[]{:S(2)}) copy-start(pred[48]{0:T(512)(128)(4,1)} %compare_and_fusion.2) | copy-start | bytes 148
  169.7 25.8 %copy-start.15 = (bf16[48,96]{1,0:T(8,128)(2,1)S(1)}, bf16[48,96]{1,0:T(8,128)(2,1)}, u32[]{:S(2)}) copy-start(bf16[48,96]{1,0:T(8,128)(2,1)} %param.24) | copy-start | bytes 27652
  170.7 36.5 %copy-start.2 = (s32[32,32,32]{1,0,2:T(8,128)S(1)}, s32[32,32,32]{1,0,2:T(8,128)}, u32[]{:S(2)}) copy-start(s32[32,32,32]{1,0,2:T(8,128)} %copy.196) | copy-start | bytes 393220
  170.7 36.5 %copy-start.7 = (pred[32,32,32]{1,0,2:T(8,128)(4,1)S(1)}, pred[32,32,32]{1,0,2:T(8,128)(4,1)}, u32[]{:S(2)}) copy-start(pred[32,32,32]{1,0,2:T(8,128)(4,1)} %copy.194) | copy-start | bytes 98308
  196.6 22.2 %all-to-all-start.3 = ((f32[32,32,96]{2,1,0:T(8,128)}), f32[32,32,96]{2,1,0:T(8,128)S(1)}, u32[]{:S(2)}, u32[]{:S(2)}) async-start(f32[32,32,96]{2,1,0:T(8,128)} %bitcast.26), calls=%async_computation.3 | async-start | bytes 1048576 | tf_op jit(solution)/shard_map/all_to_all | solution.py:21
  208.2 1.0 copy-start.5
  276.5 5.2 %copy-start.25 = (f32[1536]{0:T(1024)S(1)}, f32[1536]{0:T(1024)}, u32[]{:S(2)}) copy-start(f32[1536]{0:T(1024)} %param.30) | copy-start | bytes 18436
  280.1 3.2 copy-start.10
  283.7 6.3 %copy-start.4 = (pred[32,32,32]{2,1,0:T(8,128)(4,1)S(1)}, pred[32,32,32]{2,1,0:T(8,128)(4,1)}, u32[]{:S(2)}) copy-start(pred[32,32,32]{2,1,0:T(8,128)(4,1)} %copy-done.3) | copy-start | bytes 98308
  283.7 7.6 %copy-start.1 = (bf16[32,8,1536]{2,1,0:T(8,128)(2,1)S(1)}, bf16[32,8,1536]{2,1,0:T(8,128)(2,1)}, u32[]{:S(2)}) copy-start(bf16[32,8,1536]{2,1,0:T(8,128)(2,1)} %copy.200) | copy-start | bytes 2359300
  283.7 7.6 %copy-start.24 = (bf16[1536,32]{0,1:T(8,128)(2,1)S(1)}, bf16[1536,32]{0,1:T(8,128)(2,1)}, u32[]{:S(2)}) copy-start(bf16[1536,32]{0,1:T(8,128)(2,1)} %param.31) | copy-start | bytes 294916
  284.9 36.6 %all-to-all-start.5 = ((bf16[16,256,96]{1,2,0:T(8,128)(2,1)}), bf16[16,256,96]{1,2,0:T(8,128)(2,1)S(1)}, u32[]{:S(2)}, u32[]{:S(2)}) async-start(bf16[16,256,96]{1,2,0:T(8,128)(2,1)} %bitcast.39), calls=%async_computation.5 | async-start | bytes 1572864 | tf_op jit(solution)/shard_map/all_to_all | solution.py:21
where the time goes:
time: 343 us; the launch traced here: 342 us
  blocking collectives  189 us (55%)
  waiting for transfers between devices  58.9 us (17%)
  starting transfers between devices  37.1 us (11%)
  local copies, waits for them, and re-layouts  31.9 us (9%)
  other arithmetic  15.9 us (5%)
  matrix products  8.57 us (2%)
    all_to_all x5, waiting for transfers between devices, exchange(): return lax.all_to_all(values, axis, 0, 0, tiled=True)  58.9 us
    all_gather x1, blocking collectives, on_device(): lax.all_gather(slot_rows, 'mp', axis=2, tiled=True).reshape(n_seq * MOST, D)  45.7 us
    all_to_all x5, starting transfers between devices, exchange(): return lax.all_to_all(values, axis, 0, 0, tiled=True)  37.1 us
    all_gather x1, blocking collectives, on_device(): normed_all = lax.all_gather(normed, 'seq', axis=0, tiled=True)  32 us
    all_to_all x2, blocking collectives, exchange(): return lax.all_to_all(values, axis, 0, 0, tiled=True)  29.8 us
    all_gather x1, blocking collectives, on_device(): qkv_rows = lax.all_gather(qkv_cols, 'seq', axis=1, tiled=True)  29.1 us
    psum x1, blocking collectives, on_device(): square_sum = lax.psum(jnp.sum(x_home * x_home, axis=-1), 'mp')  27.4 us
    all_gather x1, blocking collectives, on_device(): att_all = lax.all_gather(attended, 'mp', axis=0, tiled=True)  24.4 us
  transfers between devices with their start and end apart: 5, of which 5 were waited for; matrix products, arithmetic and copies ran while one was open for 5% of the time, Pallas kernels for 0%

commit v1 on v0

--- a/solution.py
+++ b/solution.py
@@ -136,7 +136,9 @@
     denominator = jnp.sum(cache_weight * got_sum, axis=0) + own_weight * n_sum
     numerator = jnp.sum(cache_weight * got_acc, axis=0) + own_weight * n_acc
     attended = (numerator / denominator).astype(jnp.bfloat16)
-    att_all = lax.all_gather(attended, "mp", axis=0, tiled=True)
+    att_all = jnp.concatenate(
+        lax.all_to_all(jnp.stack([attended] * lax.axis_size("mp")), "mp", 0, 0), axis=0
+    )
     out_part = jnp.dot(att_all, w_out, preferred_element_type=jnp.float32)
     out_got = exchange(out_part.reshape(n_seq, home_rows, out_part.shape[-1]), "seq")
     x2 = (x_home + jnp.sum(out_got, axis=0)).astype(jnp.bfloat16)

time: 343 us -> 331 us (0.965)
  blocking collectives: 189 us -> 163 us
  waiting for transfers between devices: 58.9 us -> 72.6 us
    all_gather x1 -> x0, blocking collectives: 24.4 us -> none  [on_device(): att_all = lax.all_gather(attended, 'mp', axis=0, tiled=True)]
    all_to_all x0 -> x1, waiting for transfers between devices: none -> 10.2 us  [on_device(): lax.all_to_all(jnp.stack([attended] * lax.axis_size('mp')), 'mp', 0, 0)]
    all_to_all x5, starting transfers between devices: 37.1 us -> 30.5 us  [exchange(): return lax.all_to_all(values, axis, 0, 0, tiled=True)]
    all_to_all x0 -> x1, starting transfers between devices: none -> 5.83 us  [on_device(): lax.all_to_all(jnp.stack([attended] * lax.axis_size('mp')), 'mp', 0, 0)]
    all_to_all x5, waiting for transfers between devices: 58.9 us -> 62.3 us  [exchange(): return lax.all_to_all(values, axis, 0, 0, tiled=True)]
  transfers between devices with their start and end apart: 5 -> 6, of which waited for: 5 -> 6; matrix products, arithmetic and copies ran while one was open for 5% -> 5% of each run, Pallas kernels for 0% -> 0%
where the time goes in v1:
time: 331 us; the launch traced here: 329 us
  blocking collectives  163 us (49%)
  waiting for transfers between devices  72.6 us (22%)
  starting transfers between devices  36.3 us (11%)
  local copies, waits for them, and re-layouts  32.3 us (10%)
  other arithmetic  16 us (5%)
  matrix products  8.53 us (3%)
    all_to_all x5, waiting for transfers between devices, exchange(): return lax.all_to_all(values, axis, 0, 0, tiled=True)  62.3 us
    all_gather x1, blocking collectives, on_device(): lax.all_gather(slot_rows, 'mp', axis=2, tiled=True).reshape(n_seq * MOST, D)  46.6 us
    all_to_all x5, starting transfers between devices, exchange(): return lax.all_to_all(values, axis, 0, 0, tiled=True)  30.5 us
    all_gather x1, blocking collectives, on_device(): normed_all = lax.all_gather(normed, 'seq', axis=0, tiled=True)  30.2 us
    all_to_all x2, blocking collectives, exchange(): return lax.all_to_all(values, axis, 0, 0, tiled=True)  29.8 us
    all_gather x1, blocking collectives, on_device(): qkv_rows = lax.all_gather(qkv_cols, 'seq', axis=1, tiled=True)  28.8 us
    psum x1, blocking collectives, on_device(): square_sum = lax.psum(jnp.sum(x_home * x_home, axis=-1), 'mp')  27.4 us
    all_to_all x1, waiting for transfers between devices, on_device(): lax.all_to_all(jnp.stack([attended] * lax.axis_size('mp')), 'mp', 0, 0)  10.2 us
  transfers between devices with their start and end apart: 6, of which 6 were waited for; matrix products, arithmetic and copies ran while one was open for 5% of the time, Pallas kernels for 0%

profile of v1, /device:TPU:1, one launch (start us, length us, event | category | flops | bytes accessed | tf_op | source)
XLA Modules:
  0.0 329.5 jit_solution(2485919629909847429)
XLA Ops:
  0.0 0.7 compare_and_fusion.1
  0.7 0.7 subtract_clamp_fusion
  2.2 2.2 copy.149
  4.4 3.2 gather_fusion
  7.6 1.0 select_select_fusion
  8.7 10.4 %all-to-all-start = ((bf16[32,32,96]{2,1,0:T(8,128)(2,1)}), bf16[32,32,96]{2,1,0:T(8,128)(2,1)S(1)}, u32[]{:S(2)}, u32[]{:S(2)}) async-start(bf16[32,32,96]{2,1,0:T(8,128)(2,1)} %select_select_fusion), calls=%async_computation | async-start | bytes 524288 | tf_op jit(solution)/shard_map/all_to_all | solution.py:21
  22.9 1.3 broadcast_select_fusion.2
  24.2 3.9 %all-to-all-done = bf16[32,32,96]{2,1,0:T(8,128)(2,1)S(1)} async-done(((bf16[32,32,96]{2,1,0:T(8,128)(2,1)}), bf16[32,32,96]{2,1,0:T(8,128)(2,1)S(1)}, u32[]{:S(2)}, u32[]{:S(2)}) %all-to-all-start) | async-done | bytes 196640 | tf_op jit(solution)/shard_map/all_to_all | solution.py:21
  28.3 27.4 %psum.7 = f32[32]{0:T(128)S(1)} all-reduce(f32[32]{0:T(128)S(1)} %multiply_reduce_fusion.2), channel_id=1, replica_groups=mesh['seq'=32,'mp'=16] {'mp'}, use_global_device_ids=true, to_apply=%region_2.3 | all-reduce | flops 32 | bytes 256 | tf_op jit(solution)/shard_map/psum | solution.py:54
  55.7 30.2 %all_gather.9 = bf16[1024,96]{1,0:T(8,128)(2,1)S(1)} all-gather(bf16[32,96]{1,0:T(8,128)(2,1)S(1)} %multiply_convert_fusion), channel_id=1, replica_groups=mesh['seq'=32,'mp'=16] {'seq'}, dimensions={0}, use_global_device_ids=true | all-gather | bytes 202752 | tf_op jit(solution)/shard_map/all_gather | solution.py:56
  86.5 1.0 reshape.314
  87.5 6.4 %all-to-all-start.1 = ((f32[16,1,4096]{2,1,0:T(1,128)}), f32[16,1,4096]{2,1,0:T(1,128)S(1)}, u32[]{:S(2)}, u32[]{:S(2)}) async-start(f32[16,1,4096]{2,1,0:T(1,128)} %reshape.314), calls=%async_computation.1 | async-start | bytes 524288 | tf_op jit(solution)/shard_map/all_to_all | solution.py:21
  94.9 13.2 %all-to-all-done.1 = f32[16,1,4096]{2,1,0:T(1,128)S(1)} async-done(((f32[16,1,4096]{2,1,0:T(1,128)}), f32[16,1,4096]{2,1,0:T(1,128)S(1)}, u32[]{:S(2)}, u32[]{:S(2)}) %all-to-all-start.1) | async-done | bytes 262176 | tf_op jit(solution)/shard_map/all_to_all | solution.py:21
  108.7 1.2 reduce.3
  110.2 28.8 %all_gather.10 = bf16[64,2048]{0,1:T(8,128)(2,1)S(1)} all-gather(bf16[64,64]{0,1:T(8,128)(2,1)S(1)} %bitcast_reduce_fusion), channel_id=1, replica_groups=mesh['seq'=32,'mp'=16] {'seq'}, dimensions={1}, use_global_device_ids=true | all-gather | bytes 270336 | tf_op jit(solution)/shard_map/all_gather | solution.py:61
  140.8 0.8 fusion.77
  145.1 1.0 copy.166
  146.0 1.0 copy.163
  147.0 1.6 pad_maximum_fusion
  148.6 1.8 copy.167
  150.5 1.3 reshape.316
  151.8 4.3 %all-to-all-start.2 = ((f32[32,1,3328]{2,1,0:T(1,128)}), f32[32,1,3328]{2,1,0:T(1,128)S(1)}, u32[]{:S(2)}, u32[]{:S(2)}) async-start(f32[32,1,3328]{2,1,0:T(1,128)} %reshape.316), calls=%async_computation.2 | async-start | bytes 851968 | tf_op jit(solution)/shard_map/all_to_all | solution.py:21
  156.1 1.3 fusion.78
  158.6 0.7 gather_fusion.4
  159.3 0.7 gather_fusion.3
  160.7 5.9 %all-to-all-done.2 = f32[32,1,3328]{2,1,0:T(1,128)S(1)} async-done(((f32[32,1,3328]{2,1,0:T(1,128)}), f32[32,1,3328]{2,1,0:T(1,128)S(1)}, u32[]{:S(2)}, u32[]{:S(2)}) %all-to-all-start.2) | async-done | bytes 426016 | tf_op jit(solution)/shard_map/all_to_all | solution.py:21
  166.6 1.6 reduce.4
  169.4 0.8 reshape.318
  170.2 5.8 %all-to-all-start.3 = ((bf16[16,2,1536]{2,1,0:T(2,128)(2,1)}), bf16[16,2,1536]{2,1,0:T(2,128)(2,1)S(1)}, u32[]{:S(2)}, u32[]{:S(2)}) async-start(bf16[16,2,1536]{2,1,0:T(2,128)(2,1)} %reshape.318), calls=%async_computation.3 | async-start | bytes 196608 | tf_op jit(solution)/shard_map/all_to_all | solution.py:140
  176.0 0.8 fusion.1
  178.1 10.2 %all-to-all-done.3 = bf16[16,2,1536]{2,1,0:T(2,128)(2,1)S(1)} async-done(((bf16[16,2,1536]{2,1,0:T(2,128)(2,1)}), bf16[16,2,1536]{2,1,0:T(2,128)(2,1)S(1)}, u32[]{:S(2)}, u32[]{:S(2)}) %all-to-all-start.3) | async-done | bytes 98336 | tf_op jit(solution)/shard_map/all_to_all | solution.py:140
  188.7 1.0 fusion.63
  189.7 5.4 %all-to-all-start.4 = ((f32[32,32,96]{2,1,0:T(8,128)}), f32[32,32,96]{2,1,0:T(8,128)S(1)}, u32[]{:S(2)}, u32[]{:S(2)}) async-start(f32[32,32,96]{2,1,0:T(8,128)} %fusion.63), calls=%async_computation.4 | async-start | bytes 1048576 | tf_op jit(solution)/shard_map/all_to_all | solution.py:21
  195.1 0.9 fusion
  196.0 0.9 copy-done.4
  197.1 9.6 %all-to-all-done.4 = f32[32,32,96]{2,1,0:T(8,128)S(1)} async-done(((f32[32,32,96]{2,1,0:T(8,128)}), f32[32,32,96]{2,1,0:T(8,128)S(1)}, u32[]{:S(2)}, u32[]{:S(2)}) %all-to-all-start.4) | async-done | bytes 393248 | tf_op jit(solution)/shard_map/all_to_all | solution.py:21
  207.0 10.8 %all_to_all.40 = bf16[32,8,96]{2,1,0:T(8,128)(2,1)S(1)} all-to-all(bf16[32,8,96]{2,1,0:T(8,128)(2,1)S(1)} %copy.196), channel_id=1, replica_groups=mesh['seq'=32,'mp'=16] {'seq'}, dimensions={0} | all-to-all | bytes 98304 | tf_op jit(solution)/shard_map/all_to_all | solution.py:21
  217.8 0.8 copy.197
  218.6 46.6 %all_gather.11 = bf16[32,8,1536]{0,1,2:T(8,128)(2,1)S(1)} all-gather(bf16[32,8,96]{0,1,2:T(8,128)(2,1)} %copy.197), channel_id=1, replica_groups=mesh['seq'=32,'mp'=16] {'mp'}, dimensions={2}, use_global_device_ids=true | all-gather | bytes 835584 | tf_op jit(solution)/shard_map/all_gather | solution.py:158
  265.2 3.6 %copy.198 = bf16[32,8,1536]{2,1,0:T(8,128)(2,1)} copy(bf16[32,8,1536]{0,1,2:T(8,128)(2,1)S(1)} %all_gather.11) | data formatting | bytes 1572864 | tf_op jit(solution)/shard_map/all_gather | solution.py:158
  268.9 1.4 fusion.5
  270.5 1.6 fusion.24
  272.5 1.2 copy.203
  273.6 4.1 %all-to-all-start.6 = ((bf16[16,256,96]{1,2,0:T(8,128)(2,1)}), bf16[16,256,96]{1,2,0:T(8,128)(2,1)S(1)}, u32[]{:S(2)}, u32[]{:S(2)}) async-start(bf16[16,256,96]{1,2,0:T(8,128)(2,1)} %bitcast.39), calls=%async_computation.6 | async-start | bytes 1572864 | tf_op jit(solution)/shard_map/all_to_all | solution.py:21
  277.8 1.0 multiply_reduce_fusion
  279.7 29.7 %all-to-all-done.6 = bf16[16,256,96]{1,2,0:T(8,128)(2,1)S(1)} async-done(((bf16[16,256,96]{1,2,0:T(8,128)(2,1)}), bf16[16,256,96]{1,2,0:T(8,128)(2,1)S(1)}, u32[]{:S(2)}, u32[]{:S(2)}) %all-to-all-start.6) | async-done | bytes 786464 | tf_op jit(solution)/shard_map/all_to_all | solution.py:21
  309.7 19.0 %all_to_all.41 = bf16[32,8,96]{2,1,0:T(8,128)(2,1)S(1)} all-to-all(bf16[32,8,96]{2,1,0:T(8,128)(2,1)S(1)} %fusion.46), channel_id=1, replica_groups=mesh['seq'=32,'mp'=16] {'seq'}, dimensions={0} | all-to-all | bytes 98304 | tf_op jit(solution)/shard_map/all_to_all | solution.py:21
  328.7 0.8 fusion.13
  (159 shorter events, 18.8 us)
Async XLA Ops:
  0.0 270.5 %copy-start = (bf16[1,2,48,1536]{3,2,1,0:T(8,128)(2,1)S(1)}, bf16[1,2,48,1536]{3,2,1,0:T(8,128)(2,1)}, u32[]{:S(2)}) copy-start(bf16[1,2,48,1536]{3,2,1,0:T(8,128)(2,1)} %param.32) | copy-start | bytes 884740
  4.4 16.3 %copy-start.18 = (s32[2]{0:T(128)S(1)}, s32[2]{0:T(128)}, u32[]{:S(2)}) copy-start(s32[2]{0:T(128)} %param.28) | copy-start | bytes 28
  4.4 17.0 %copy-start.10 = (bf16[2,2,64,256]{3,2,1,0:T(8,128)(2,1)S(1)}, bf16[2,2,64,256]{3,2,1,0:T(8,128)(2,1)}, u32[]{:S(2)}) copy-start(bf16[2,2,64,256]{3,2,1,0:T(8,128)(2,1)} %param.25) | copy-start | bytes 393220
  4.4 17.1 %copy-start.12 = (s32[256,4,4]{0,2,1:T(4,128)S(1)}, s32[256,4,4]{0,2,1:T(4,128)}, u32[]{:S(2)}) copy-start(s32[256,4,4]{0,2,1:T(4,128)} %param.34) | copy-start | bytes 49156
  7.6 14.4 %copy-start.5 = (bf16[2,16,64,256]{3,2,1,0:T(8,128)(2,1)S(1)}, bf16[2,16,64,256]{3,2,1,0:T(8,128)(2,1)}, u32[]{:S(2)}) copy-start(bf16[2,16,64,256]{3,2,1,0:T(8,128)(2,1)} %param.26) | copy-start | bytes 3145732
  8.7 19.4 %all-to-all-start = ((bf16[32,32,96]{2,1,0:T(8,128)(2,1)}), bf16[32,32,96]{2,1,0:T(8,128)(2,1)S(1)}, u32[]{:S(2)}, u32[]{:S(2)}) async-start(bf16[32,32,96]{2,1,0:T(8,128)(2,1)} %select_select_fusion), calls=%async_computation | async-start | bytes 524288 | tf_op jit(solution)/shard_map/all_to_all | solution.py:21
  22.2 0.7 copy-start.21
  22.2 33.4 %copy-start.19 = (f32[96]{0:T(128)S(1)}, f32[96]{0:T(128)}, u32[]{:S(2)}) copy-start(f32[96]{0:T(128)} %param.22) | copy-start | bytes 1156
  22.4 63.6 %copy-start.13 = (bf16[96,64]{0,1:T(8,128)(2,1)S(1)}, bf16[96,64]{0,1:T(8,128)(2,1)}, u32[]{:S(2)}) copy-start(bf16[96,64]{0,1:T(8,128)(2,1)} %param.23) | copy-start | bytes 36868
  86.2 7.8 %copy-start.22 = (s32[16]{0:T(128)S(1)}, s32[16]{0:T(128)}, u32[]{:S(2)}) copy-start(s32[16]{0:T(128)} %param.29) | copy-start | bytes 196
  86.2 8.6 %copy-start.20 = (s32[64]{0:T(128)S(1)}, s32[64]{0:T(128)}, u32[]{:S(2)}) copy-start(s32[64]{0:T(128)} %constant.117) | copy-start | bytes 772
  87.5 20.6 %all-to-all-start.1 = ((f32[16,1,4096]{2,1,0:T(1,128)}), f32[16,1,4096]{2,1,0:T(1,128)S(1)}, u32[]{:S(2)}, u32[]{:S(2)}) async-start(f32[16,1,4096]{2,1,0:T(1,128)} %reshape.314), calls=%async_computation.1 | async-start | bytes 524288 | tf_op jit(solution)/shard_map/all_to_all | solution.py:21
  140.8 1.6 copy-start.6
  150.5 5.6 %copy-start.7 = (bf16[16,4,2,6,128]{4,3,2,1,0:T(8,128)(2,1)S(1)}, bf16[16,4,2,6,128]{4,3,2,1,0:T(8,128)(2,1)}, u32[]{:S(2)}) copy-start(bf16[16,4,2,6,128]{4,3,2,1,0:T(8,128)(2,1)} %copy-done.6) | copy-start | bytes 589828
  150.5 5.6 %copy-start.11 = (bf16[16,4,2,128]{3,2,1,0:T(2,128)(2,1)S(1)}, bf16[16,4,2,128]{3,2,1,0:T(2,128)(2,1)}, u32[]{:S(2)}) copy-start(bf16[16,4,2,128]{3,2,1,0:T(2,128)(2,1)} %reshape.246) | copy-start | bytes 98308
  150.5 5.6 %copy-start.16 = (pred[4,4]{1,0:T(4,128)(4,1)S(1)}, pred[4,4]{1,0:T(4,128)(4,1)}, u32[]{:S(2)}) copy-start(pred[4,4]{1,0:T(4,128)(4,1)} %iota_compare_fusion.2) | copy-start | bytes 52
  150.5 7.5 %copy-start.8 = (bf16[64,256]{0,1:T(8,128)(2,1)S(1)}, bf16[64,256]{0,1:T(8,128)(2,1)}, u32[]{:S(2)}) copy-start(bf16[64,256]{0,1:T(8,128)(2,1)} %get-tuple-element.16) | copy-start | bytes 98308
  151.8 14.9 %all-to-all-start.2 = ((f32[32,1,3328]{2,1,0:T(1,128)}), f32[32,1,3328]{2,1,0:T(1,128)S(1)}, u32[]{:S(2)}, u32[]{:S(2)}) async-start(f32[32,1,3328]{2,1,0:T(1,128)} %reshape.316), calls=%async_computation.2 | async-start | bytes 851968 | tf_op jit(solution)/shard_map/all_to_all | solution.py:21
  160.4 8.2 %copy-start.17 = (pred[48]{0:T(512)(128)(4,1)S(1)}, pred[48]{0:T(512)(128)(4,1)}, u32[]{:S(2)}) copy-start(pred[48]{0:T(512)(128)(4,1)} %subtract_compare_fusion) | copy-start | bytes 148
  160.4 8.3 %copy-start.15 = (pred[48]{0:T(512)(128)(4,1)S(1)}, pred[48]{0:T(512)(128)(4,1)}, u32[]{:S(2)}) copy-start(pred[48]{0:T(512)(128)(4,1)} %compare_and_fusion.2) | copy-start | bytes 148
  170.2 18.5 %copy-start.14 = (bf16[48,96]{1,0:T(8,128)(2,1)S(1)}, bf16[48,96]{1,0:T(8,128)(2,1)}, u32[]{:S(2)}) copy-start(bf16[48,96]{1,0:T(8,128)(2,1)} %param.24) | copy-start | bytes 27652
  170.2 18.1 %all-to-all-start.3 = ((bf16[16,2,1536]{2,1,0:T(2,128)(2,1)}), bf16[16,2,1536]{2,1,0:T(2,128)(2,1)S(1)}, u32[]{:S(2)}, u32[]{:S(2)}) async-start(bf16[16,2,1536]{2,1,0:T(2,128)(2,1)} %reshape.318), calls=%async_computation.3 | async-start | bytes 196608 | tf_op jit(solution)/shard_map/all_to_all | solution.py:140
  176.8 0.6 copy-start.2
  189.7 17.0 %all-to-all-start.4 = ((f32[32,32,96]{2,1,0:T(8,128)}), f32[32,32,96]{2,1,0:T(8,128)S(1)}, u32[]{:S(2)}, u32[]{:S(2)}) async-start(f32[32,32,96]{2,1,0:T(8,128)} %fusion.63), calls=%async_computation.4 | async-start | bytes 1048576 | tf_op jit(solution)/shard_map/all_to_all | solution.py:21
  196.0 1.0 copy-start.4
  265.2 5.2 %copy-start.24 = (f32[1536]{0:T(1024)S(1)}, f32[1536]{0:T(1024)}, u32[]{:S(2)}) copy-start(f32[1536]{0:T(1024)} %param.30) | copy-start | bytes 18436
  268.9 3.2 copy-start.9
  272.4 5.3 %copy-start.3 = (pred[32,32,32]{2,1,0:T(8,128)(4,1)S(1)}, pred[32,32,32]{2,1,0:T(8,128)(4,1)}, u32[]{:S(2)}) copy-start(pred[32,32,32]{2,1,0:T(8,128)(4,1)} %copy-done.2) | copy-start | bytes 98308
  272.5 6.5 %copy-start.1 = (bf16[32,8,1536]{2,1,0:T(8,128)(2,1)S(1)}, bf16[32,8,1536]{2,1,0:T(8,128)(2,1)}, u32[]{:S(2)}) copy-start(bf16[32,8,1536]{2,1,0:T(8,128)(2,1)} %copy.198) | copy-start | bytes 2359300
  272.5 6.5 %copy-start.23 = (bf16[1536,32]{0,1:T(8,128)(2,1)S(1)}, bf16[1536,32]{0,1:T(8,128)(2,1)}, u32[]{:S(2)}) copy-start(bf16[1536,32]{0,1:T(8,128)(2,1)} %param.31) | copy-start | bytes 294916
  273.6 35.7 %all-to-all-start.6 = ((bf16[16,256,96]{1,2,0:T(8,128)(2,1)}), bf16[16,256,96]{1,2,0:T(8,128)(2,1)S(1)}, u32[]{:S(2)}, u32[]{:S(2)}) async-start(bf16[16,256,96]{1,2,0:T(8,128)(2,1)} %bitcast.39), calls=%async_computation.6 | async-start | bytes 1572864 | tf_op jit(solution)/shard_map/all_to_all | solution.py:21
